TPU v7x, 256 devices: a whole 4x4x8 slice. The times are simulated.
256 devices in a mesh: tm: 16 (over y, x), space: 16 (over z, core).
Axes of the slice: x: 4, y: 4, z: 8, core: 2. Of those that a mesh axis runs over, the one named last changes fastest.
Arguments:
- stored: bfloat16 [16, 288, 128, 128], P('tm', None, 'space'), may hold values from -6 to 6
- snapshot: int32 [16, 256], P('tm'), may hold values from 0 to 287, as said below
- balance_coef: float32 [128, 128], P('space'), may hold values from 0.5 to 2
- sea_mask: int32 [128, 128], P('space'), may hold values 0 or 1
Outputs:
- merged_basis: bfloat16 [256, 3, 128, 128], P('tm', None, 'space')
Inputs may be any that keep to these rules, and one draw needn't show every extreme that they name: `snapshot`: the 256 indices of one group are distinct.
All inputs are finite; a program needn't handle non-finite values. No bound on the sum of `sea_mask` on one device may be relied on, other than what follows from the above.
Results may differ from a plain program's by a relative error of at most 0.04.
Values may be sent and summed in bfloat16 or wider, within the bound.
No kernel may reach another device: no remote copies, remote signals or barrier semaphores. Data moves between devices by JAX's collectives and lax.ppermute only.
A program may use at most 64 MiB of HBM per device.

v0:
```python
import jax
import jax.numpy as jnp
from jax import lax
from jax.sharding import PartitionSpec as P

inv_root2 = 0.7071067811865476


def gathered_total(shard, axis):
    return lax.all_gather(shard, axis).astype(jnp.float32).sum(0)


def with_halo(cells, sides, width):
    for axis, dim in sides:
        count = lax.axis_size(axis)
        ends = count - 1
        head = lax.slice_in_dim(cells, 0, width, axis=dim)
        tail = lax.slice_in_dim(cells, cells.shape[dim] - width, cells.shape[dim], axis=dim)
        cells = jnp.concatenate(
            [
                lax.ppermute(tail, axis, [(i, (i + 1) % count) for i in range(ends)]),
                cells,
                lax.ppermute(head, axis, [((i + 1) % count, i) for i in range(ends)]),
            ],
            axis=dim,
        )
    return cells


def from_partner(shard, axis, stride):
    return lax.ppermute(shard, axis, [(i, i ^ 1 << stride) for i in range(lax.axis_size(axis))])


def balance(padded, balance_coef, sea_float):
    center = padded[:, 1:-1, :]
    values = center.astype(jnp.float32)
    east_cells = jnp.roll(values, -1, axis=2)
    west_cells = jnp.roll(values, 1, axis=2)
    zonal_flow = (-balance_coef * sea_float * (east_cells - west_cells)).astype(jnp.bfloat16)
    wide = padded.astype(jnp.float32)
    merid_flow = (balance_coef * sea_float * (wide[:, 2:, :] - wide[:, :-2, :])).astype(
        jnp.bfloat16
    )
    return jnp.stack([center, zonal_flow, merid_flow], axis=1).reshape(center.shape[0], -1)


def stack_pair(own_basis, other_basis, level_idx):
    own_bit = lax.axis_index("tm") // 2**level_idx % 2
    upper_part = jnp.where(own_bit == 0, own_basis, other_basis)
    lower_part = jnp.where(own_bit == 0, other_basis, own_basis)
    return jnp.concatenate([upper_part, lower_part], axis=0)


def merge_pair(own_basis, other_basis, level_idx, last_level):
    stacked = stack_pair(own_basis, other_basis, level_idx)
    members = own_basis.shape[0]
    local_gram = jnp.dot(stacked, stacked.T, preferred_element_type=jnp.float32)
    local_mixed = (local_gram[:, :members] + local_gram[:, members:]) * inv_root2
    mixed_cols = lax.psum(local_mixed, "space")
    normal = jnp.dot(
        mixed_cols.T,
        mixed_cols,
        precision=lax.Precision.HIGHEST,
        preferred_element_type=jnp.float32,
    )
    factor_low = jnp.linalg.cholesky(normal)
    rotation = (
        jax.scipy.linalg.solve_triangular(factor_low, mixed_cols.T, lower=True) * inv_root2
    ).astype(jnp.bfloat16)
    if last_level:
        member_share = rotation.shape[0] // lax.axis_size("tm")
        rotation = lax.dynamic_slice_in_dim(
            rotation, lax.axis_index("tm") * member_share, member_share, 0
        )
    return jnp.dot(rotation, stacked, preferred_element_type=jnp.float32).astype(jnp.bfloat16)


def body(stored, snapshot, balance_coef, sea_mask):
    sea_float = sea_mask.astype(jnp.float32)
    mean_state = jnp.mean(stored[0].astype(jnp.float32), axis=0)
    picked = jnp.take(stored[0], snapshot[0], axis=0)
    anomaly = ((picked.astype(jnp.float32) - mean_state) * sea_float).astype(jnp.bfloat16)
    padded = with_halo(anomaly, (("space", 1),), 1)
    basis_now = balance(padded, balance_coef, sea_float)
    levels = lax.axis_size("tm").bit_length() - 1
    first_level = 0
    other_padded = from_partner(padded, "tm", 0)
    partner = balance(other_padded, balance_coef, sea_float)
    basis_now = merge_pair(basis_now, partner, 0, levels == 1)
    first_level = 1
    for level_idx in range(first_level, levels):
        partner = from_partner(basis_now, "tm", level_idx)
        basis_now = merge_pair(basis_now, partner, level_idx, level_idx == levels - 1)
    return basis_now.reshape(basis_now.shape[0], 3, stored.shape[2], stored.shape[3])


def solution(mesh):
    placed = (P("tm", None, "space", None), P("tm", None), P("space", None), P("space", None))
    return jax.shard_map(
        body, mesh=mesh, in_specs=placed, out_specs=P("tm", None, "space", None), check_vma=False
    )
```

profile of v0, /device:TPU:1, one launch (start us, length us, event | category | flops | bytes accessed | tf_op | source)
XLA Modules:
  0.0 906.1 jit_solution(1723753065468144391)
XLA Ops:
  12.4 5.1 collective-permute-start.1
  33.1 7.0 collective-permute-done.2
  40.1 2.9 fusion.98
  54.2 3.0 fusion.10
  61.3 3.8 fusion.3
  66.2 112.5 %all-reduce.6.cloned.1.call-done = f32[512,256]{1,0:T(8,128)} async-done(((f32[512,256]{1,0:T(8,128)}), f32[512,256]{1,0:T(8,128)}) %all-reduce.6.cloned.1.call-update) | async-done | bytes 524304 | tf_op jit(solution)/shard_map/psum | solution.py:59
  181.2 11.7 %cholesky.214 = f32[128,128]{1,0:T(8,128)S(1)} custom-call(f32[128,128]{1,0:T(8,128)S(1)} %cholesky.346), custom_call_target="Cholesky" | custom-call | tf_op jit(solution)/shard_map/jit(cholesky)/cholesky | solution.py:66
  192.9 9.8 %custom-call.17 = f32[1,128,128]{1,2,0:T(8,128)S(1)} custom-call(f32[1,128,128]{2,1,0:T(8,128)S(1)} %get-tuple-element.118), custom_call_target="InvertDiagBlocksLowerTriangular" | custom-call | tf_op jit(solution)/shard_map/jit(cholesky)/cholesky | solution.py:66
  203.2 11.7 %cholesky.231 = f32[128,128]{1,0:T(8,128)S(1)} custom-call(f32[128,128]{1,0:T(8,128)S(1)} %convolution_subtract_fusion.7), custom_call_target="Cholesky" | custom-call | tf_op jit(solution)/shard_map/jit(cholesky)/cholesky | solution.py:66
  217.7 4.2 while.8
  221.8 19.7 %custom-call.18 = f32[2,128,128]{1,2,0:T(8,128)S(1)} custom-call(f32[2,128,128]{2,1,0:T(8,128)S(1)} %get-tuple-element.33), custom_call_target="InvertDiagBlocksLowerTriangular" | custom-call | tf_op jit(solution)/shard_map/jit(_solve_triangular)/triangular_solve | solution.py:68
  246.8 34.2 %collective-permute-done.3 = bf16[256,3072]{1,0:T(8,128)(2,1)} collective-permute-done((bf16[256,3072]{1,0:T(8,128)(2,1)S(1)}, bf16[256,3072]{1,0:T(8,128)(2,1)}, u32[]{:S(2)}, u32[]{:S(2)}) %collective-permute-start.3) | collective-permute-done | bytes 1572896 | tf_op jit(solution)/shard_map/ppermute | solution.py:31
  286.3 110.5 %all-reduce.8.cloned.1.call-done = f32[512,256]{1,0:T(8,128)} async-done(((f32[512,256]{1,0:T(8,128)}), f32[512,256]{1,0:T(8,128)}) %all-reduce.8.cloned.1.call-update) | async-done | bytes 524304 | tf_op jit(solution)/shard_map/psum | solution.py:59
  399.2 11.7 %cholesky.248 = f32[128,128]{1,0:T(8,128)S(1)} custom-call(f32[128,128]{1,0:T(8,128)S(1)} %cholesky.349), custom_call_target="Cholesky" | custom-call | tf_op jit(solution)/shard_map/jit(cholesky)/cholesky | solution.py:66
  411.0 9.8 %custom-call.19 = f32[1,128,128]{1,2,0:T(8,128)S(1)} custom-call(f32[1,128,128]{2,1,0:T(8,128)S(1)} %get-tuple-element.114), custom_call_target="InvertDiagBlocksLowerTriangular" | custom-call | tf_op jit(solution)/shard_map/jit(cholesky)/cholesky | solution.py:66
  421.3 11.7 %cholesky.265 = f32[128,128]{1,0:T(8,128)S(1)} custom-call(f32[128,128]{1,0:T(8,128)S(1)} %convolution_subtract_fusion.6), custom_call_target="Cholesky" | custom-call | tf_op jit(solution)/shard_map/jit(cholesky)/cholesky | solution.py:66
  435.7 4.1 while.9
  439.8 19.7 %custom-call.20 = f32[2,128,128]{1,2,0:T(8,128)S(1)} custom-call(f32[2,128,128]{2,1,0:T(8,128)S(1)} %get-tuple-element.34), custom_call_target="InvertDiagBlocksLowerTriangular" | custom-call | tf_op jit(solution)/shard_map/jit(_solve_triangular)/triangular_solve | solution.py:68
  464.3 34.4 %collective-permute-done.4 = bf16[256,3072]{1,0:T(8,128)(2,1)} collective-permute-done((bf16[256,3072]{1,0:T(8,128)(2,1)}, bf16[256,3072]{1,0:T(8,128)(2,1)}, u32[]{:S(2)}, u32[]{:S(2)}) %collective-permute-start.4) | collective-permute-done | bytes 1572896 | tf_op jit(solution)/shard_map/ppermute | solution.py:31
  503.8 110.7 %all-reduce.10.cloned.1.call-done = f32[512,256]{1,0:T(8,128)} async-done(((f32[512,256]{1,0:T(8,128)}), f32[512,256]{1,0:T(8,128)}) %all-reduce.10.cloned.1.call-update) | async-done | bytes 524304 | tf_op jit(solution)/shard_map/psum | solution.py:59
  617.0 11.7 %cholesky.282 = f32[128,128]{1,0:T(8,128)S(1)} custom-call(f32[128,128]{1,0:T(8,128)S(1)} %cholesky.352), custom_call_target="Cholesky" | custom-call | tf_op jit(solution)/shard_map/jit(cholesky)/cholesky | solution.py:66
  628.7 9.8 %custom-call.21 = f32[1,128,128]{1,2,0:T(8,128)S(1)} custom-call(f32[1,128,128]{2,1,0:T(8,128)S(1)} %get-tuple-element.110), custom_call_target="InvertDiagBlocksLowerTriangular" | custom-call | tf_op jit(solution)/shard_map/jit(cholesky)/cholesky | solution.py:66
  639.0 11.7 %cholesky.299 = f32[128,128]{1,0:T(8,128)S(1)} custom-call(f32[128,128]{1,0:T(8,128)S(1)} %convolution_subtract_fusion.5), custom_call_target="Cholesky" | custom-call | tf_op jit(solution)/shard_map/jit(cholesky)/cholesky | solution.py:66
  653.4 4.3 while.10
  657.8 19.7 %custom-call.22 = f32[2,128,128]{1,2,0:T(8,128)S(1)} custom-call(f32[2,128,128]{2,1,0:T(8,128)S(1)} %get-tuple-element.35), custom_call_target="InvertDiagBlocksLowerTriangular" | custom-call | tf_op jit(solution)/shard_map/jit(_solve_triangular)/triangular_solve | solution.py:68
  683.8 34.4 %collective-permute-done.5 = bf16[256,3072]{1,0:T(8,128)(2,1)} collective-permute-done((bf16[256,3072]{1,0:T(8,128)(2,1)}, bf16[256,3072]{1,0:T(8,128)(2,1)}, u32[]{:S(2)}, u32[]{:S(2)}) %collective-permute-start.5) | collective-permute-done | bytes 1572896 | tf_op jit(solution)/shard_map/ppermute | solution.py:31
  723.0 111.0 %all-reduce.12.cloned.1.call-done = f32[512,256]{1,0:T(8,128)} async-done(((f32[512,256]{1,0:T(8,128)}), f32[512,256]{1,0:T(8,128)}) %all-reduce.12.cloned.1.call-update) | async-done | bytes 524304 | tf_op jit(solution)/shard_map/psum | solution.py:59
  836.4 11.7 %cholesky.316 = f32[128,128]{1,0:T(8,128)S(1)} custom-call(f32[128,128]{1,0:T(8,128)S(1)} %cholesky.355), custom_call_target="Cholesky" | custom-call | tf_op jit(solution)/shard_map/jit(cholesky)/cholesky | solution.py:66
  848.2 9.8 %custom-call.23 = f32[1,128,128]{1,2,0:T(8,128)S(1)} custom-call(f32[1,128,128]{2,1,0:T(8,128)S(1)} %get-tuple-element.106), custom_call_target="InvertDiagBlocksLowerTriangular" | custom-call | tf_op jit(solution)/shard_map/jit(cholesky)/cholesky | solution.py:66
  858.5 11.9 %cholesky.333 = f32[128,128]{1,0:T(8,128)S(1)} custom-call(f32[128,128]{1,0:T(8,128)S(1)} %convolution_subtract_fusion.4), custom_call_target="Cholesky" | custom-call | tf_op jit(solution)/shard_map/jit(cholesky)/cholesky | solution.py:66
  873.0 3.9 while.11
  877.0 19.7 %custom-call.24 = f32[2,128,128]{1,2,0:T(8,128)S(1)} custom-call(f32[2,128,128]{2,1,0:T(8,128)S(1)} %get-tuple-element.36), custom_call_target="InvertDiagBlocksLowerTriangular" | custom-call | tf_op jit(solution)/shard_map/jit(_solve_triangular)/triangular_solve | solution.py:68
  (193 shorter events, 104.6 us)
Async XLA Ops:
  6.5 172.2 %all-reduce.6.cloned.1.call-start = ((), (), s32[]{:S(2)}) async-start(), calls=%async_computation | async-start | bytes 1048576 | tf_op jit(solution)/shard_map/psum | solution.py:59
  11.9 8.1 copy-start
  12.4 7.6 collective-permute-start.1
  17.5 3.9 collective-permute-start
  23.0 17.1 %collective-permute-start.2 = (bf16[256,10,128]{2,0,1:T(8,128)(2,1)}, bf16[256,10,128]{2,0,1:T(8,128)(2,1)}, u32[]{:S(2)}, u32[]{:S(2)}) collective-permute-start(bf16[256,10,128]{2,0,1:T(8,128)(2,1)} %copy.45), channel_id=1, source_target_pairs={{0,16},{16,0},{32,48},{48,32},{64,80},{80,64},{96,112},{112,96},{1... | collective-permute-start | bytes 1966088 | tf_op jit(solution)/shard_map/ppermute | solution.py:31
  27.1 4.3 copy-start.20
  27.1 4.3 copy-start.21
  50.9 2.4 copy-start.1
  50.9 2.4 copy-start.6
  50.9 2.6 copy-start.7
  50.9 2.9 copy-start.8
  50.9 3.3 copy-start.9
  54.2 3.0 copy-start.10
  59.5 1.9 copy-start.11
  66.0 330.8 %all-reduce.8.cloned.1.call-start = ((), (), s32[]{:S(2)}) async-start(), calls=%async_computation.1 | async-start | bytes 1048576 | tf_op jit(solution)/shard_map/psum | solution.py:59
  181.1 60.4 %copy-start.3 = (f32[512,256]{1,0:T(8,128)S(1)}, f32[512,256]{1,0:T(8,128)}, u32[]{:S(2)}) copy-start(f32[512,256]{1,0:T(8,128)} %all-reduce.6.cloned.1.call-done) | copy-start | bytes 1572868
  241.5 1.5 copy-start.12
  244.0 2.8 copy-start.19
  244.0 37.0 %collective-permute-start.3 = (bf16[256,3072]{1,0:T(8,128)(2,1)S(1)}, bf16[256,3072]{1,0:T(8,128)(2,1)}, u32[]{:S(2)}, u32[]{:S(2)}) collective-permute-start(bf16[256,3072]{1,0:T(8,128)(2,1)S(1)} %convolution_convert_fusion.2), channel_id=1, source_target_pairs={{0,32},{16,48},{32,0},{48,16},{64,96},{80,112},{96,64},{112,80},{1... | collective-permute-start | bytes 4718600 | tf_op jit(solution)/shard_map/ppermute | solution.py:31
  283.1 1.8 copy-start.15
  285.8 328.7 %all-reduce.10.cloned.1.call-start = ((), (), s32[]{:S(2)}) async-start(), calls=%async_computation.2 | async-start | bytes 1048576 | tf_op jit(solution)/shard_map/psum | solution.py:59
  399.2 60.3 %copy-start.4 = (f32[512,256]{1,0:T(8,128)S(1)}, f32[512,256]{1,0:T(8,128)}, u32[]{:S(2)}) copy-start(f32[512,256]{1,0:T(8,128)} %all-reduce.8.cloned.1.call-done) | copy-start | bytes 1572868
  459.5 1.5 copy-start.16
  463.1 35.6 %collective-permute-start.4 = (bf16[256,3072]{1,0:T(8,128)(2,1)}, bf16[256,3072]{1,0:T(8,128)(2,1)}, u32[]{:S(2)}, u32[]{:S(2)}) collective-permute-start(bf16[256,3072]{1,0:T(8,128)(2,1)} %convolution_convert_fusion.1), channel_id=1, source_target_pairs={{0,64},{16,80},{32,96},{48,112},{64,0},{80,16},{96,32},{112,48},{1... | collective-permute-start | bytes 4718600 | tf_op jit(solution)/shard_map/ppermute | solution.py:31
  500.8 1.8 copy-start.17
  503.6 330.4 %all-reduce.12.cloned.1.call-start = ((), (), s32[]{:S(2)}) async-start(), calls=%async_computation.3 | async-start | bytes 1048576 | tf_op jit(solution)/shard_map/psum | solution.py:59
  616.9 60.5 %copy-start.5 = (f32[512,256]{1,0:T(8,128)S(1)}, f32[512,256]{1,0:T(8,128)}, u32[]{:S(2)}) copy-start(f32[512,256]{1,0:T(8,128)} %all-reduce.10.cloned.1.call-done) | copy-start | bytes 1572868
  677.4 1.5 copy-start.18
  681.1 37.1 %collective-permute-start.5 = (bf16[256,3072]{1,0:T(8,128)(2,1)}, bf16[256,3072]{1,0:T(8,128)(2,1)}, u32[]{:S(2)}, u32[]{:S(2)}) collective-permute-start(bf16[256,3072]{1,0:T(8,128)(2,1)} %convolution_convert_fusion), channel_id=1, source_target_pairs={{0,128},{16,144},{32,160},{48,176},{64,192},{80,208},{96,224},{112... | collective-permute-start | bytes 4718600 | tf_op jit(solution)/shard_map/ppermute | solution.py:31
  720.3 1.8 copy-start.13
  836.4 60.3 %copy-start.2 = (f32[512,256]{1,0:T(8,128)S(1)}, f32[512,256]{1,0:T(8,128)}, u32[]{:S(2)}) copy-start(f32[512,256]{1,0:T(8,128)} %all-reduce.12.cloned.1.call-done) | copy-start | bytes 1572868
  896.7 1.5 copy-start.14
Sparse Core Ops, SparseCore 0:
  66.1 112.5 all-reduce.5
  286.0 110.8 all-reduce.7
  503.7 110.8 all-reduce.9
  723.1 110.8 all-reduce.11
where the time goes:
time: 914 us; the launch traced here: 906 us
  waiting for transfers between devices  557 us (61%)
  other arithmetic  241 us (26%)
  local copies, waits for them, and re-layouts  40.6 us (4%)
  matrix products  31.5 us (3%)
  between operations  19.1 us (2%)
  starting transfers between devices  15.7 us (2%)
    psum x4, waiting for transfers between devices, merge_pair(): mixed_cols = lax.psum(local_mixed, 'space')  445 us
    another operation x28, other arithmetic, merge_pair(): factor_low = jnp.linalg.cholesky(normal)  139 us
    ppermute x4, waiting for transfers between devices, from_partner(): lax.ppermute(shard, axis, [(i, i ^ 1 << stride) for i in range(lax.axis_s...  110 us
    another operation x9, other arithmetic, merge_pair(): jax.scipy.linalg.solve_triangular(factor_low, mixed_cols.T, lower=True)  78.8 us
  transfers between devices with their start and end apart: 10, of which 10 were waited for; matrix products, arithmetic and copies ran while one was open for 1% of the time, Pallas kernels for 0%

commit v1 on v0

--- a/solution.py
+++ b/solution.py
@@ -56,7 +56,11 @@
     members = own_basis.shape[0]
     local_gram = jnp.dot(stacked, stacked.T, preferred_element_type=jnp.float32)
     local_mixed = (local_gram[:, :members] + local_gram[:, members:]) * inv_root2
-    mixed_cols = lax.psum(local_mixed, "space")
+    mixed_cols = local_mixed
+    for hop in (1, 2, 4, 8):
+        mixed_cols = mixed_cols + lax.ppermute(
+            mixed_cols, "space", [(dev, dev ^ hop) for dev in range(16)]
+        )
     normal = jnp.dot(
         mixed_cols.T,
         mixed_cols,

time: 914 us -> 735 us (0.80)
  waiting for transfers between devices: 557 us -> 358 us
  starting transfers between devices: 15.7 us -> 51.8 us
  between operations: 19.1 us -> 6.54 us
    psum x4 -> x0, waiting for transfers between devices: 445 us -> none  [merge_pair(): mixed_cols = lax.psum(local_mixed, 'space')]
    ppermute x0 -> x16, waiting for transfers between devices: none -> 248 us  [merge_pair(): lax.ppermute(mixed_cols, 'space', [(dev, dev ^ hop) for dev in range(16)])]
    ppermute x0 -> x16, starting transfers between devices: none -> 36.7 us  [merge_pair(): lax.ppermute(mixed_cols, 'space', [(dev, dev ^ hop) for dev in range(16)])]
  transfers between devices with their start and end apart: 10 -> 22, of which waited for: 10 -> 22; matrix products, arithmetic and copies ran while one was open for 1% -> 1% of each run, Pallas kernels for 0% -> 0%
where the time goes in v1:
time: 735 us; the launch traced here: 725 us
  waiting for transfers between devices  358 us (49%)
  other arithmetic  240 us (33%)
  starting transfers between devices  51.8 us (7%)
  local copies, waits for them, and re-layouts  41.3 us (6%)
  matrix products  26.9 us (4%)
    ppermute x16, waiting for transfers between devices, merge_pair(): lax.ppermute(mixed_cols, 'space', [(dev, dev ^ hop) for dev in range(16)])  248 us
    another operation x28, other arithmetic, merge_pair(): factor_low = jnp.linalg.cholesky(normal)  139 us
    ppermute x4, waiting for transfers between devices, from_partner(): lax.ppermute(shard, axis, [(i, i ^ 1 << stride) for i in range(lax.axis_s...  108 us
    another operation x9, other arithmetic, merge_pair(): jax.scipy.linalg.solve_triangular(factor_low, mixed_cols.T, lower=True)  78.8 us
    ppermute x16, starting transfers between devices, merge_pair(): lax.ppermute(mixed_cols, 'space', [(dev, dev ^ hop) for dev in range(16)])  36.7 us
    another operation x29, local copies, waits for them, and re-layouts, merge_pair(): jax.scipy.linalg.solve_triangular(factor_low, mixed_cols.T, lower=True)  16.4 us
  transfers between devices with their start and end apart: 22, of which 22 were waited for; matrix products, arithmetic and copies ran while one was open for 1% of the time, Pallas kernels for 0%

profile of v1, /device:TPU:1, one launch (start us, length us, event | category | flops | bytes accessed | tf_op | source)
XLA Modules:
  0.0 725.4 jit_solution(9073866080178970670)
XLA Ops:
  26.6 7.0 collective-permute-done.2
  62.4 11.6 %collective-permute-done.4 = f32[512,256]{1,0:T(8,128)S(1)} collective-permute-done((f32[512,256]{1,0:T(8,128)S(1)}, f32[512,256]{1,0:T(8,128)S(1)}, u32[]{:S(2)}, u32[]{:S(2)}) %collective-permute-start.4) | collective-permute-done | bytes 524320 | tf_op jit(solution)/shard_map/ppermute | solution.py:61
  78.9 22.7 %collective-permute-done.5 = f32[512,256]{1,0:T(8,128)S(1)} collective-permute-done((f32[512,256]{1,0:T(8,128)S(1)}, f32[512,256]{1,0:T(8,128)S(1)}, u32[]{:S(2)}, u32[]{:S(2)}) %collective-permute-start.5) | collective-permute-done | bytes 524320 | tf_op jit(solution)/shard_map/ppermute | solution.py:61
  106.4 23.0 %collective-permute-done.6 = f32[512,256]{1,0:T(8,128)S(1)} collective-permute-done((f32[512,256]{1,0:T(8,128)S(1)}, f32[512,256]{1,0:T(8,128)S(1)}, u32[]{:S(2)}, u32[]{:S(2)}) %collective-permute-start.6) | collective-permute-done | bytes 524320 | tf_op jit(solution)/shard_map/ppermute | solution.py:61
  130.6 11.7 %cholesky.214 = f32[128,128]{1,0:T(8,128)S(1)} custom-call(f32[128,128]{1,0:T(8,128)S(1)} %cholesky.346), custom_call_target="Cholesky" | custom-call | tf_op jit(solution)/shard_map/jit(cholesky)/cholesky | solution.py:70
  142.4 9.8 %custom-call.17 = f32[1,128,128]{1,2,0:T(8,128)S(1)} custom-call(f32[1,128,128]{2,1,0:T(8,128)S(1)} %get-tuple-element.118), custom_call_target="InvertDiagBlocksLowerTriangular" | custom-call | tf_op jit(solution)/shard_map/jit(cholesky)/cholesky | solution.py:70
  152.7 11.7 %cholesky.231 = f32[128,128]{1,0:T(8,128)S(1)} custom-call(f32[128,128]{1,0:T(8,128)S(1)} %slice_subtract_fusion.13), custom_call_target="Cholesky" | custom-call | tf_op jit(solution)/shard_map/jit(cholesky)/cholesky | solution.py:70
  171.8 19.7 %custom-call.18 = f32[2,128,128]{1,2,0:T(8,128)S(1)} custom-call(f32[2,128,128]{2,1,0:T(8,128)S(1)} %get-tuple-element.33), custom_call_target="InvertDiagBlocksLowerTriangular" | custom-call | tf_op jit(solution)/shard_map/jit(_solve_triangular)/triangular_solve | solution.py:72
  197.0 32.8 %collective-permute-done.7 = bf16[256,3072]{1,0:T(8,128)(2,1)} collective-permute-done((bf16[256,3072]{1,0:T(8,128)(2,1)S(1)}, bf16[256,3072]{1,0:T(8,128)(2,1)}, u32[]{:S(2)}, u32[]{:S(2)}) %collective-permute-start.7) | collective-permute-done | bytes 1572896 | tf_op jit(solution)/shard_map/ppermute | solution.py:31
  238.5 13.1 %collective-permute-done.9 = f32[512,256]{1,0:T(8,128)S(1)} collective-permute-done((f32[512,256]{1,0:T(8,128)S(1)}, f32[512,256]{1,0:T(8,128)S(1)}, u32[]{:S(2)}, u32[]{:S(2)}) %collective-permute-start.9) | collective-permute-done | bytes 524320 | tf_op jit(solution)/shard_map/ppermute | solution.py:61
  254.5 22.7 %collective-permute-done.10 = f32[512,256]{1,0:T(8,128)S(1)} collective-permute-done((f32[512,256]{1,0:T(8,128)S(1)}, f32[512,256]{1,0:T(8,128)S(1)}, u32[]{:S(2)}, u32[]{:S(2)}) %collective-permute-start.10) | collective-permute-done | bytes 524320 | tf_op jit(solution)/shard_map/ppermute | solution.py:61
  281.0 25.2 %collective-permute-done.11 = f32[512,256]{1,0:T(8,128)S(1)} collective-permute-done((f32[512,256]{1,0:T(8,128)S(1)}, f32[512,256]{1,0:T(8,128)S(1)}, u32[]{:S(2)}, u32[]{:S(2)}) %collective-permute-start.11) | collective-permute-done | bytes 524320 | tf_op jit(solution)/shard_map/ppermute | solution.py:61
  307.4 11.7 %cholesky.248 = f32[128,128]{1,0:T(8,128)S(1)} custom-call(f32[128,128]{1,0:T(8,128)S(1)} %cholesky.349), custom_call_target="Cholesky" | custom-call | tf_op jit(solution)/shard_map/jit(cholesky)/cholesky | solution.py:70
  319.1 9.8 %custom-call.19 = f32[1,128,128]{1,2,0:T(8,128)S(1)} custom-call(f32[1,128,128]{2,1,0:T(8,128)S(1)} %get-tuple-element.114), custom_call_target="InvertDiagBlocksLowerTriangular" | custom-call | tf_op jit(solution)/shard_map/jit(cholesky)/cholesky | solution.py:70
  329.4 11.7 %cholesky.265 = f32[128,128]{1,0:T(8,128)S(1)} custom-call(f32[128,128]{1,0:T(8,128)S(1)} %slice_subtract_fusion.12), custom_call_target="Cholesky" | custom-call | tf_op jit(solution)/shard_map/jit(cholesky)/cholesky | solution.py:70
  348.3 19.7 %custom-call.20 = f32[2,128,128]{1,2,0:T(8,128)S(1)} custom-call(f32[2,128,128]{2,1,0:T(8,128)S(1)} %get-tuple-element.34), custom_call_target="InvertDiagBlocksLowerTriangular" | custom-call | tf_op jit(solution)/shard_map/jit(_solve_triangular)/triangular_solve | solution.py:72
  373.0 34.2 %collective-permute-done.12 = bf16[256,3072]{1,0:T(8,128)(2,1)} collective-permute-done((bf16[256,3072]{1,0:T(8,128)(2,1)}, bf16[256,3072]{1,0:T(8,128)(2,1)}, u32[]{:S(2)}, u32[]{:S(2)}) %collective-permute-start.12) | collective-permute-done | bytes 1572896 | tf_op jit(solution)/shard_map/ppermute | solution.py:31
  414.7 13.1 %collective-permute-done.14 = f32[512,256]{1,0:T(8,128)S(1)} collective-permute-done((f32[512,256]{1,0:T(8,128)S(1)}, f32[512,256]{1,0:T(8,128)S(1)}, u32[]{:S(2)}, u32[]{:S(2)}) %collective-permute-start.14) | collective-permute-done | bytes 524320 | tf_op jit(solution)/shard_map/ppermute | solution.py:61
  430.5 22.7 %collective-permute-done.15 = f32[512,256]{1,0:T(8,128)S(1)} collective-permute-done((f32[512,256]{1,0:T(8,128)S(1)}, f32[512,256]{1,0:T(8,128)S(1)}, u32[]{:S(2)}, u32[]{:S(2)}) %collective-permute-start.15) | collective-permute-done | bytes 524320 | tf_op jit(solution)/shard_map/ppermute | solution.py:61
  456.7 25.9 %collective-permute-done.16 = f32[512,256]{1,0:T(8,128)S(1)} collective-permute-done((f32[512,256]{1,0:T(8,128)S(1)}, f32[512,256]{1,0:T(8,128)S(1)}, u32[]{:S(2)}, u32[]{:S(2)}) %collective-permute-start.16) | collective-permute-done | bytes 524320 | tf_op jit(solution)/shard_map/ppermute | solution.py:61
  483.8 11.7 %cholesky.282 = f32[128,128]{1,0:T(8,128)S(1)} custom-call(f32[128,128]{1,0:T(8,128)S(1)} %cholesky.352), custom_call_target="Cholesky" | custom-call | tf_op jit(solution)/shard_map/jit(cholesky)/cholesky | solution.py:70
  495.5 9.8 %custom-call.21 = f32[1,128,128]{1,2,0:T(8,128)S(1)} custom-call(f32[1,128,128]{2,1,0:T(8,128)S(1)} %get-tuple-element.110), custom_call_target="InvertDiagBlocksLowerTriangular" | custom-call | tf_op jit(solution)/shard_map/jit(cholesky)/cholesky | solution.py:70
  505.8 11.7 %cholesky.299 = f32[128,128]{1,0:T(8,128)S(1)} custom-call(f32[128,128]{1,0:T(8,128)S(1)} %slice_subtract_fusion.11), custom_call_target="Cholesky" | custom-call | tf_op jit(solution)/shard_map/jit(cholesky)/cholesky | solution.py:70
  524.7 19.7 %custom-call.22 = f32[2,128,128]{1,2,0:T(8,128)S(1)} custom-call(f32[2,128,128]{2,1,0:T(8,128)S(1)} %get-tuple-element.35), custom_call_target="InvertDiagBlocksLowerTriangular" | custom-call | tf_op jit(solution)/shard_map/jit(_solve_triangular)/triangular_solve | solution.py:72
  551.1 34.3 %collective-permute-done.17 = bf16[256,3072]{1,0:T(8,128)(2,1)} collective-permute-done((bf16[256,3072]{1,0:T(8,128)(2,1)}, bf16[256,3072]{1,0:T(8,128)(2,1)}, u32[]{:S(2)}, u32[]{:S(2)}) %collective-permute-start.17) | collective-permute-done | bytes 1572896 | tf_op jit(solution)/shard_map/ppermute | solution.py:31
  592.6 13.1 %collective-permute-done.19 = f32[512,256]{1,0:T(8,128)S(1)} collective-permute-done((f32[512,256]{1,0:T(8,128)S(1)}, f32[512,256]{1,0:T(8,128)S(1)}, u32[]{:S(2)}, u32[]{:S(2)}) %collective-permute-start.19) | collective-permute-done | bytes 524320 | tf_op jit(solution)/shard_map/ppermute | solution.py:61
  609.1 22.7 %collective-permute-done.20 = f32[512,256]{1,0:T(8,128)S(1)} collective-permute-done((f32[512,256]{1,0:T(8,128)S(1)}, f32[512,256]{1,0:T(8,128)S(1)}, u32[]{:S(2)}, u32[]{:S(2)}) %collective-permute-start.20) | collective-permute-done | bytes 524320 | tf_op jit(solution)/shard_map/ppermute | solution.py:61
  634.7 25.9 %collective-permute-done.21 = f32[512,256]{1,0:T(8,128)S(1)} collective-permute-done((f32[512,256]{1,0:T(8,128)S(1)}, f32[512,256]{1,0:T(8,128)S(1)}, u32[]{:S(2)}, u32[]{:S(2)}) %collective-permute-start.21) | collective-permute-done | bytes 524320 | tf_op jit(solution)/shard_map/ppermute | solution.py:61
  661.8 11.7 %cholesky.316 = f32[128,128]{1,0:T(8,128)S(1)} custom-call(f32[128,128]{1,0:T(8,128)S(1)} %cholesky.355), custom_call_target="Cholesky" | custom-call | tf_op jit(solution)/shard_map/jit(cholesky)/cholesky | solution.py:70
  673.6 9.8 %custom-call.23 = f32[1,128,128]{1,2,0:T(8,128)S(1)} custom-call(f32[1,128,128]{2,1,0:T(8,128)S(1)} %get-tuple-element.106), custom_call_target="InvertDiagBlocksLowerTriangular" | custom-call | tf_op jit(solution)/shard_map/jit(cholesky)/cholesky | solution.py:70
  683.9 11.7 %cholesky.333 = f32[128,128]{1,0:T(8,128)S(1)} custom-call(f32[128,128]{1,0:T(8,128)S(1)} %slice_subtract_fusion.10), custom_call_target="Cholesky" | custom-call | tf_op jit(solution)/shard_map/jit(cholesky)/cholesky | solution.py:70
  702.6 19.7 %custom-call.24 = f32[2,128,128]{1,2,0:T(8,128)S(1)} custom-call(f32[2,128,128]{2,1,0:T(8,128)S(1)} %get-tuple-element.36), custom_call_target="InvertDiagBlocksLowerTriangular" | custom-call | tf_op jit(solution)/shard_map/jit(_solve_triangular)/triangular_solve | solution.py:72
  (221 shorter events, 173.5 us)
Async XLA Ops:
  5.3 8.1 %copy-start = (bf16[256,8,128]{2,1,0:T(8,128)(2,1)}, bf16[256,8,128]{2,1,0:T(8,128)(2,1)S(1)}, u32[]{:S(2)}) copy-start(bf16[256,8,128]{2,1,0:T(8,128)(2,1)S(1)} %gather_fusion) | copy-start | bytes 1572868
  5.9 7.6 %collective-permute-start.1 = (bf16[256,1,128]{2,1,0:T(2,128)(2,1)S(1)}, bf16[256,1,128]{2,1,0:T(2,128)(2,1)S(1)}, u32[]{:S(2)}, u32[]{:S(2)}) collective-permute-start(bf16[256,1,128]{2,1,0:T(2,128)(2,1)S(1)} %get-tuple-element.102), channel_id=1, source_target_pairs={{1,0},{2,1},{3,2},{4,3},{5,4},{6,5},{7,6},{8,7},{9,8},{10,9},{11,1... | collective-permute-start | bytes 196616 | tf_op jit(solution)/shard_map/ppermute | solution.py:23
  11.0 3.9 collective-permute-start
  16.5 17.1 %collective-permute-start.2 = (bf16[256,10,128]{2,0,1:T(8,128)(2,1)}, bf16[256,10,128]{2,0,1:T(8,128)(2,1)}, u32[]{:S(2)}, u32[]{:S(2)}) collective-permute-start(bf16[256,10,128]{2,0,1:T(8,128)(2,1)} %copy.45), channel_id=1, source_target_pairs={{0,16},{16,0},{32,48},{48,32},{64,80},{80,64},{96,112},{112,96},{1... | collective-permute-start | bytes 1966088 | tf_op jit(solution)/shard_map/ppermute | solution.py:31
  20.6 4.3 copy-start.16
  20.6 4.3 copy-start.17
  44.4 2.4 copy-start.1
  44.4 2.4 copy-start.2
  44.4 2.6 copy-start.3
  44.4 2.9 copy-start.4
  44.4 3.3 copy-start.5
  47.7 3.0 copy-start.6
  58.7 2.0 collective-permute-start.3
  60.9 13.2 %collective-permute-start.4 = (f32[512,256]{1,0:T(8,128)S(1)}, f32[512,256]{1,0:T(8,128)S(1)}, u32[]{:S(2)}, u32[]{:S(2)}) collective-permute-start(f32[512,256]{1,0:T(8,128)S(1)} %fusion.128), channel_id=1, source_target_pairs={{0,2},{1,3},{2,0},{3,1},{4,6},{5,7},{6,4},{7,5},{8,10},{9,11},{10,... | collective-permute-start | bytes 1572872 | tf_op jit(solution)/shard_map/ppermute | solution.py:61
  74.1 27.5 %collective-permute-start.5 = (f32[512,256]{1,0:T(8,128)S(1)}, f32[512,256]{1,0:T(8,128)S(1)}, u32[]{:S(2)}, u32[]{:S(2)}) collective-permute-start(f32[512,256]{1,0:T(8,128)S(1)} %add.129), channel_id=1, source_target_pairs={{0,4},{1,5},{2,6},{3,7},{4,0},{5,1},{6,2},{7,3},{8,12},{9,13},{10,... | collective-permute-start | bytes 1572872 | tf_op jit(solution)/shard_map/ppermute | solution.py:61
  101.7 27.7 %collective-permute-start.6 = (f32[512,256]{1,0:T(8,128)S(1)}, f32[512,256]{1,0:T(8,128)S(1)}, u32[]{:S(2)}, u32[]{:S(2)}) collective-permute-start(f32[512,256]{1,0:T(8,128)S(1)} %add.130), channel_id=1, source_target_pairs={{0,8},{1,9},{2,10},{3,11},{4,12},{5,13},{6,14},{7,15},{8,0},{9,1},... | collective-permute-start | bytes 1572872 | tf_op jit(solution)/shard_map/ppermute | solution.py:61
  194.1 2.9 copy-start.15
  194.1 35.6 %collective-permute-start.7 = (bf16[256,3072]{1,0:T(8,128)(2,1)S(1)}, bf16[256,3072]{1,0:T(8,128)(2,1)}, u32[]{:S(2)}, u32[]{:S(2)}) collective-permute-start(bf16[256,3072]{1,0:T(8,128)(2,1)S(1)} %convolution_convert_fusion.2), channel_id=1, source_target_pairs={{0,32},{16,48},{32,0},{48,16},{64,96},{80,112},{96,64},{112,80},{1... | collective-permute-start | bytes 4718600 | tf_op jit(solution)/shard_map/ppermute | solution.py:31
  233.7 4.5 collective-permute-start.8
  238.4 13.2 %collective-permute-start.9 = (f32[512,256]{1,0:T(8,128)S(1)}, f32[512,256]{1,0:T(8,128)S(1)}, u32[]{:S(2)}, u32[]{:S(2)}) collective-permute-start(f32[512,256]{1,0:T(8,128)S(1)} %fusion.127), channel_id=1, source_target_pairs={{0,2},{1,3},{2,0},{3,1},{4,6},{5,7},{6,4},{7,5},{8,10},{9,11},{10,... | collective-permute-start | bytes 1572872 | tf_op jit(solution)/shard_map/ppermute | solution.py:61
  251.6 25.6 %collective-permute-start.10 = (f32[512,256]{1,0:T(8,128)S(1)}, f32[512,256]{1,0:T(8,128)S(1)}, u32[]{:S(2)}, u32[]{:S(2)}) collective-permute-start(f32[512,256]{1,0:T(8,128)S(1)} %add.134), channel_id=1, source_target_pairs={{0,4},{1,5},{2,6},{3,7},{4,0},{5,1},{6,2},{7,3},{8,12},{9,13},{10,... | collective-permute-start | bytes 1572872 | tf_op jit(solution)/shard_map/ppermute | solution.py:61
  277.3 28.9 %collective-permute-start.11 = (f32[512,256]{1,0:T(8,128)S(1)}, f32[512,256]{1,0:T(8,128)S(1)}, u32[]{:S(2)}, u32[]{:S(2)}) collective-permute-start(f32[512,256]{1,0:T(8,128)S(1)} %add.135), channel_id=1, source_target_pairs={{0,8},{1,9},{2,10},{3,11},{4,12},{5,13},{6,14},{7,15},{8,0},{9,1},... | collective-permute-start | bytes 1572872 | tf_op jit(solution)/shard_map/ppermute | solution.py:61
  371.8 35.4 %collective-permute-start.12 = (bf16[256,3072]{1,0:T(8,128)(2,1)}, bf16[256,3072]{1,0:T(8,128)(2,1)}, u32[]{:S(2)}, u32[]{:S(2)}) collective-permute-start(bf16[256,3072]{1,0:T(8,128)(2,1)} %convolution_convert_fusion.1), channel_id=1, source_target_pairs={{0,64},{16,80},{32,96},{48,112},{64,0},{80,16},{96,32},{112,48},{1... | collective-permute-start | bytes 4718600 | tf_op jit(solution)/shard_map/ppermute | solution.py:31
  411.2 3.3 collective-permute-start.13
  414.6 13.2 %collective-permute-start.14 = (f32[512,256]{1,0:T(8,128)S(1)}, f32[512,256]{1,0:T(8,128)S(1)}, u32[]{:S(2)}, u32[]{:S(2)}) collective-permute-start(f32[512,256]{1,0:T(8,128)S(1)} %fusion.126), channel_id=1, source_target_pairs={{0,2},{1,3},{2,0},{3,1},{4,6},{5,7},{6,4},{7,5},{8,10},{9,11},{10,... | collective-permute-start | bytes 1572872 | tf_op jit(solution)/shard_map/ppermute | solution.py:61
  427.9 25.4 %collective-permute-start.15 = (f32[512,256]{1,0:T(8,128)S(1)}, f32[512,256]{1,0:T(8,128)S(1)}, u32[]{:S(2)}, u32[]{:S(2)}) collective-permute-start(f32[512,256]{1,0:T(8,128)S(1)} %add.139), channel_id=1, source_target_pairs={{0,4},{1,5},{2,6},{3,7},{4,0},{5,1},{6,2},{7,3},{8,12},{9,13},{10,... | collective-permute-start | bytes 1572872 | tf_op jit(solution)/shard_map/ppermute | solution.py:61
  453.3 29.2 %collective-permute-start.16 = (f32[512,256]{1,0:T(8,128)S(1)}, f32[512,256]{1,0:T(8,128)S(1)}, u32[]{:S(2)}, u32[]{:S(2)}) collective-permute-start(f32[512,256]{1,0:T(8,128)S(1)} %add.140), channel_id=1, source_target_pairs={{0,8},{1,9},{2,10},{3,11},{4,12},{5,13},{6,14},{7,15},{8,0},{9,1},... | collective-permute-start | bytes 1572872 | tf_op jit(solution)/shard_map/ppermute | solution.py:61
  548.1 37.3 %collective-permute-start.17 = (bf16[256,3072]{1,0:T(8,128)(2,1)}, bf16[256,3072]{1,0:T(8,128)(2,1)}, u32[]{:S(2)}, u32[]{:S(2)}) collective-permute-start(bf16[256,3072]{1,0:T(8,128)(2,1)} %convolution_convert_fusion), channel_id=1, source_target_pairs={{0,128},{16,144},{32,160},{48,176},{64,192},{80,208},{96,224},{112... | collective-permute-start | bytes 4718600 | tf_op jit(solution)/shard_map/ppermute | solution.py:31
  589.4 3.0 collective-permute-start.18
  592.5 13.2 %collective-permute-start.19 = (f32[512,256]{1,0:T(8,128)S(1)}, f32[512,256]{1,0:T(8,128)S(1)}, u32[]{:S(2)}, u32[]{:S(2)}) collective-permute-start(f32[512,256]{1,0:T(8,128)S(1)} %fusion.125), channel_id=1, source_target_pairs={{0,2},{1,3},{2,0},{3,1},{4,6},{5,7},{6,4},{7,5},{8,10},{9,11},{10,... | collective-permute-start | bytes 1572872 | tf_op jit(solution)/shard_map/ppermute | solution.py:61
  605.8 26.1 %collective-permute-start.20 = (f32[512,256]{1,0:T(8,128)S(1)}, f32[512,256]{1,0:T(8,128)S(1)}, u32[]{:S(2)}, u32[]{:S(2)}) collective-permute-start(f32[512,256]{1,0:T(8,128)S(1)} %add.144), channel_id=1, source_target_pairs={{0,4},{1,5},{2,6},{3,7},{4,0},{5,1},{6,2},{7,3},{8,12},{9,13},{10,... | collective-permute-start | bytes 1572872 | tf_op jit(solution)/shard_map/ppermute | solution.py:61
  631.9 28.7 %collective-permute-start.21 = (f32[512,256]{1,0:T(8,128)S(1)}, f32[512,256]{1,0:T(8,128)S(1)}, u32[]{:S(2)}, u32[]{:S(2)}) collective-permute-start(f32[512,256]{1,0:T(8,128)S(1)} %add.145), channel_id=1, source_target_pairs={{0,8},{1,9},{2,10},{3,11},{4,12},{5,13},{6,14},{7,15},{8,0},{9,1},... | collective-permute-start | bytes 1572872 | tf_op jit(solution)/shard_map/ppermute | solution.py:61
  (8 other events, 13.6 us)
